TPU v7x, 128 devices: a whole 4x4x4 slice. The times are simulated.
128 devices in a mesh: tm: 4 (over x), space: 16 (over z, y), ens: 2 (over core).
Axes of the slice: x: 4, y: 4, z: 4, core: 2. Of those that a mesh axis runs over, the one named last changes fastest.
Arguments:
- start_states: float32 [4, 16, 1024, 1024], P('tm', 'ens', 'space'), may hold values from -6 to 6
- velocity_x: float32 [1024, 1024], P('space'), may hold values from -0.15 to 0.15
- velocity_y: float32 [1024, 1024], P('space'), may hold values from -0.15 to 0.15
- diffusivity: float32 [1024, 1024], P('space'), may hold values from 0.06 to 0.2
- source_shape: float32 [1024, 1024], P('space'), may hold values from -6 to 6
- params: float32 [16, 128], P('ens'), may hold values from -6 to 6
- obs_cell: int32 [4, 1024], P('tm', 'space'), may hold values from 0 to 1048575, as said below
- obs_data: float32 [4, 1024], P('tm', 'space'), may hold values from -6 to 6
- obs_noise: float32 [4, 1024, 16], P('tm', 'space'), may hold values from -6 to 6
- obs_var: float32 [4, 1024], P('tm', 'space'), may hold values from 0.05 to 0.5
Outputs:
- new_states: float32 [4, 16, 1024, 1024], P('tm', 'ens', 'space')
- new_params: float32 [16, 128], P('ens')
Inputs may be any that keep to these rules, and one draw needn't show every extreme that they name: `obs_cell`: entry (n, o) lies in the rows of slab o // 64, that is row (o // 64) * 64 up to 63 rows further.
All inputs are finite; a program needn't handle non-finite values.
Results may differ from a plain program's by a relative error of at most 0.0003.
Values sent between devices are 32-bit elements; how exact they have to be, the bound alone decides.
No kernel may reach another device: no remote copies, remote signals or barrier semaphores. Data moves between devices by JAX's collectives and lax.ppermute only.
A program may use at most 128 MiB of HBM per device.

v0:
```python
import math
import jax
import jax.numpy as jnp
from jax import lax
from jax.sharding import PartitionSpec as P

FINE = 4
FINE_DT = 0.25


def with_halo(cells, sides, width):
    for axis, dim in sides:
        count = lax.axis_size(axis)
        ends = count - 1
        head = lax.slice_in_dim(cells, 0, width, axis=dim)
        tail = lax.slice_in_dim(cells, cells.shape[dim] - width, cells.shape[dim], axis=dim)
        cells = jnp.concatenate(
            [
                lax.ppermute(tail, axis, [(i, (i + 1) % count) for i in range(ends)]),
                cells,
                lax.ppermute(head, axis, [((i + 1) % count, i) for i in range(ends)]),
            ],
            axis=dim,
        )
    return cells


def shifted(value, axis, steps):
    count = lax.axis_size(axis)
    first, last = (max(0, -steps), min(count, count - steps))
    return lax.ppermute(value, axis, [(source, source + steps) for source in range(first, last)])


def advance(values_in, coeffs, inside, step_size, forcing):
    middle = values_in[:, 1:-1, :]
    above_row = values_in[:, :-2, :]
    below_row = values_in[:, 2:, :]
    west_cell = jnp.pad(middle[:, :, :-1], ((0, 0), (0, 0), (1, 0)))
    east_cell = jnp.pad(middle[:, :, 1:], ((0, 0), (0, 0), (0, 1)))
    spread_term = coeffs[0] * (above_row + below_row + west_cell + east_cell - 4.0 * middle)
    tendency = (
        spread_term
        - coeffs[1] * (east_cell - west_cell) * 0.5
        - coeffs[2] * (below_row - above_row) * 0.5
    )
    if forcing is not None:
        tendency = tendency + forcing
    return (middle + step_size * tendency) * inside


def row_inside(first_row, count, total_rows):
    global_rows = first_row + jnp.arange(count, dtype=jnp.int32)
    return ((global_rows >= 0) & (global_rows < total_rows)).astype(jnp.float32)[:, None]


def per_device(
    start_states,
    velocity_x,
    velocity_y,
    diffusivity,
    source_shape,
    params,
    obs_cell,
    obs_data,
    obs_noise,
    obs_var,
):
    coarse_dt = FINE_DT * FINE
    state = start_states[0]
    members_here, row_count, col_count = state.shape
    slabs = row_count * lax.axis_size("space")
    first_row = lax.axis_index("space") * row_count
    slice_index = lax.axis_index("tm")
    band_width = col_count // params.shape[1]
    spread_params = jnp.repeat(params, band_width, axis=1)
    coeffs = jnp.stack([diffusivity, velocity_x, velocity_y])
    own_rows = row_inside(first_row, row_count, slabs)
    forcing = source_shape[None] * spread_params[:, None, :]
    current = state
    coarse_part = state
    for section in range(FINE):
        padded = with_halo(current, (("space", 1),), 1)
        if section == 0:
            coarse_part = advance(padded, coeffs, own_rows, coarse_dt, None)
        current = advance(padded, coeffs, own_rows, FINE_DT, forcing)
    correction = jnp.where(slice_index > 0, current - coarse_part, current)
    running = correction
    for link in range(lax.axis_size("tm") - 1):
        earlier = shifted(running, "tm", 1)
        padded = with_halo(earlier, (("space", 1),), 1)
        running = correction + advance(padded, coeffs, own_rows, coarse_dt, None)
    new_states = running[None]
    flat = running.reshape(members_here, row_count * col_count)
    local_cell = obs_cell[0] - first_row * col_count
    predicted = jnp.take(flat, local_cell, axis=1)
    every_pred, every_param = (
        lax.all_gather(predicted, "ens", axis=0, tiled=True),
        lax.all_gather(params, "ens", axis=0, tiled=True),
    )
    total = every_pred.shape[0]
    norm_factor = 1.0 / math.sqrt(total - 1)
    inv_spread = lax.rsqrt(obs_var[0])[None, :]
    pred_mean = jnp.mean(every_pred, axis=0, keepdims=True)
    anomaly = (every_pred - pred_mean) * (inv_spread * norm_factor)
    misfit = (obs_data[0][None, :] + obs_noise[0].T - every_pred) * inv_spread
    gram = jnp.dot(anomaly, anomaly.T, precision=lax.Precision.HIGHEST)
    cross = jnp.dot(anomaly, misfit.T, precision=lax.Precision.HIGHEST)
    gram, cross = lax.psum((gram, cross), ("tm", "space"))
    system = jnp.eye(total, dtype=jnp.float32) + gram
    factor = jnp.linalg.cholesky(system)
    weights = jax.scipy.linalg.cho_solve((factor, True), cross)
    param_anom = every_param - jnp.mean(every_param, axis=0)
    own_weights = lax.dynamic_slice_in_dim(
        weights, lax.axis_index("ens") * members_here, members_here, 1
    )
    new_params = (
        params + jnp.dot(own_weights.T, param_anom, precision=lax.Precision.HIGHEST) * norm_factor
    )
    return (new_states, new_params)


def solution(mesh):
    in_specs = (
        P("tm", "ens", "space", None),
        P("space", None),
        P("space", None),
        P("space", None),
        P("space", None),
        P("ens", None),
        P("tm", "space"),
        P("tm", "space"),
        P("tm", "space", None),
        P("tm", "space"),
    )
    out_specs = (P("tm", "ens", "space", None), P("ens", None))
    return jax.shard_map(
        per_device, mesh=mesh, in_specs=in_specs, out_specs=out_specs, check_vma=False
    )
```

profile of v0, /device:TPU:0, one launch (start us, length us, event | category | flops | bytes accessed | tf_op | source)
XLA Modules:
  0.0 608.6 jit_solution(10801937823309952952)
XLA Ops:
  1.7 3.6 collective-permute-start
  6.7 5.1 fusion.52
  14.2 3.4 fusion.2
  17.7 4.5 collective-permute-start.2
  24.4 3.7 collective-permute-done.3
  30.2 3.5 collective-permute-start.4
  35.8 4.6 collective-permute-done.5
  42.6 6.0 collective-permute-start.6
  51.0 3.7 collective-permute-done.7
  54.7 4.7 subtract_select_fusion
  59.4 3.5 collective-permute-start.8
  63.0 40.2 %collective-permute-done.8 = f32[8,64,1024]{2,1,0:T(8,128)S(1)} collective-permute-done((f32[8,64,1024]{2,1,0:T(8,128)S(1)}, f32[8,64,1024]{2,1,0:T(8,128)S(1)}, u32[]{:S(2)}, u32[]{:S(2)}) %collective-permute-start.8) | collective-permute-done | bytes 2097184 | tf_op jit(solution)/shard_map/ppermute | solution.py:31
  104.5 5.2 collective-permute-start.9
  113.2 4.7 collective-permute-start.11
  117.9 38.7 %collective-permute-done.11 = f32[8,64,1024]{2,1,0:T(8,128)S(1)} collective-permute-done((f32[8,64,1024]{2,1,0:T(8,128)S(1)}, f32[8,64,1024]{2,1,0:T(8,128)S(1)}, u32[]{:S(2)}, u32[]{:S(2)}) %collective-permute-start.11) | collective-permute-done | bytes 2097184 | tf_op jit(solution)/shard_map/ppermute | solution.py:31
  156.7 3.9 collective-permute-start.12
  162.8 3.7 collective-permute-done.13
  169.5 4.5 collective-permute-start.14
  175.9 34.7 %collective-permute-done.14 = f32[8,64,1024]{2,1,0:T(8,128)S(1)} collective-permute-done((f32[8,64,1024]{2,1,0:T(8,128)}, f32[8,64,1024]{2,1,0:T(8,128)S(1)}, u32[]{:S(2)}, u32[]{:S(2)}) %collective-permute-start.14) | collective-permute-done | bytes 2097184 | tf_op jit(solution)/shard_map/ppermute | solution.py:31
  210.6 5.4 collective-permute-start.15
  218.2 5.6 collective-permute-done.16
  226.7 17.9 %copy.18 = f32[8,64,1024]{0,2,1:T(8,128)} copy(f32[8,64,1024]{2,1,0:T(8,128)} %multiply_add_fusion.4) | data formatting | bytes 4194304 | tf_op jit(solution)/shard_map/add | solution.py:91
  244.6 11.1 %gather_fusion = f32[64,8]{1,0:T(8,128)S(1)} fusion(f32[8,65536]{0,1:T(8,128)} %bitcast.43, s32[1024]{0:T(1024)S(1)} %pad_clamp_fusion), kind=kCustom, calls=%fused_computation | custom fusion | bytes 4352 | tf_op jit(solution)/shard_map/jit(_take)/gather | solution.py:95
  258.0 345.3 %all-reduce.14 = (f32[16,16]{1,0:T(8,128)S(1)}, f32[16,16]{1,0:T(8,128)S(1)}) all-reduce(f32[16,16]{1,0:T(8,128)S(1)} %fusion.21, f32[16,16]{1,0:T(8,128)S(1)} %fusion.29), channel_id=1, replica_groups=mesh['tm'=4,'space'=16,'ens'=2] {'tm','space'}, use_global_device_ids=true, to_apply=%region_4.5 | all-reduce | flops 512 | bytes 4096 | tf_op jit(solution)/shard_map/psum | solution.py:108
  (90 shorter events, 40.2 us)
Async XLA Ops:
  1.7 12.4 %collective-permute-start = (f32[8,1,1024]{2,1,0:T(1,128)S(1)}, f32[8,1,1024]{2,1,0:T(1,128)S(1)}, u32[]{:S(2)}, u32[]{:S(2)}) collective-permute-start(f32[8,1,1024]{2,1,0:T(1,128)S(1)} %get-tuple-element.31), channel_id=1, source_target_pairs={{0,2},{2,4},{4,6},{6,8},{8,10},{10,12},{12,14},{14,16},{16,18},{18... | collective-permute-start | bytes 98312 | tf_op jit(solution)/shard_map/ppermute | solution.py:19
  5.3 8.9 %collective-permute-start.1 = (f32[8,1,1024]{2,1,0:T(1,128)S(1)}, f32[8,1,1024]{2,1,0:T(1,128)S(1)}, u32[]{:S(2)}, u32[]{:S(2)}) collective-permute-start(f32[8,1,1024]{2,1,0:T(1,128)S(1)} %get-tuple-element.30), channel_id=1, source_target_pairs={{2,0},{4,2},{6,4},{8,6},{10,8},{12,10},{14,12},{16,14},{18,16},{20... | collective-permute-start | bytes 98312 | tf_op jit(solution)/shard_map/ppermute | solution.py:21
  6.6 7.6 %copy-start = (f32[1,8,64,1024]{3,2,1,0:T(8,128)S(1)}, f32[1,8,64,1024]{3,2,1,0:T(8,128)}, u32[]{:S(2)}) copy-start(f32[1,8,64,1024]{3,2,1,0:T(8,128)} %param.10) | copy-start | bytes 6291460
  17.7 6.7 %collective-permute-start.2 = (f32[8,1,1024]{2,1,0:T(1,128)S(1)}, f32[8,1,1024]{2,1,0:T(1,128)S(1)}, u32[]{:S(2)}, u32[]{:S(2)}) collective-permute-start(f32[8,1,1024]{2,1,0:T(1,128)S(1)} %get-tuple-element.25), channel_id=1, source_target_pairs={{0,2},{2,4},{4,6},{6,8},{8,10},{10,12},{12,14},{14,16},{16,18},{18... | collective-permute-start | bytes 98312 | tf_op jit(solution)/shard_map/ppermute | solution.py:19
  22.3 5.8 collective-permute-start.3
  30.2 5.6 collective-permute-start.4
  33.7 6.8 %collective-permute-start.5 = (f32[8,1,1024]{2,1,0:T(1,128)S(1)}, f32[8,1,1024]{2,1,0:T(1,128)S(1)}, u32[]{:S(2)}, u32[]{:S(2)}) collective-permute-start(f32[8,1,1024]{2,1,0:T(1,128)S(1)} %get-tuple-element.20), channel_id=1, source_target_pairs={{2,0},{4,2},{6,4},{8,6},{10,8},{12,10},{14,12},{16,14},{18,16},{20... | collective-permute-start | bytes 98312 | tf_op jit(solution)/shard_map/ppermute | solution.py:21
  42.6 8.5 %collective-permute-start.6 = (f32[8,1,1024]{2,1,0:T(1,128)S(1)}, f32[8,1,1024]{2,1,0:T(1,128)S(1)}, u32[]{:S(2)}, u32[]{:S(2)}) collective-permute-start(f32[8,1,1024]{2,1,0:T(1,128)S(1)} %get-tuple-element.17), channel_id=1, source_target_pairs={{0,2},{2,4},{4,6},{6,8},{8,10},{10,12},{12,14},{14,16},{16,18},{18... | collective-permute-start | bytes 98312 | tf_op jit(solution)/shard_map/ppermute | solution.py:19
  48.6 6.1 collective-permute-start.7
  59.4 107.1 %copy-start.1 = (f32[8,64,1024]{2,1,0:T(8,128)}, f32[8,64,1024]{2,1,0:T(8,128)S(1)}, u32[]{:S(2)}) copy-start(f32[8,64,1024]{2,1,0:T(8,128)S(1)} %subtract_select_fusion) | copy-start | bytes 6291460
  59.4 43.7 %collective-permute-start.8 = (f32[8,64,1024]{2,1,0:T(8,128)S(1)}, f32[8,64,1024]{2,1,0:T(8,128)S(1)}, u32[]{:S(2)}, u32[]{:S(2)}) collective-permute-start(f32[8,64,1024]{2,1,0:T(8,128)S(1)} %subtract_select_fusion), channel_id=1, source_target_pairs={{0,32},{32,64},{64,96},{1,33},{33,65},{65,97},{2,34},{34,66},{66,9... | collective-permute-start | bytes 6291464 | tf_op jit(solution)/shard_map/ppermute | solution.py:31
  103.2 7.3 %collective-permute-start.10 = (f32[8,1,1024]{2,1,0:T(1,128)S(1)}, f32[8,1,1024]{2,1,0:T(1,128)S(1)}, u32[]{:S(2)}, u32[]{:S(2)}) collective-permute-start(f32[8,1,1024]{2,1,0:T(1,128)S(1)} %get-tuple-element.12), channel_id=1, source_target_pairs={{2,0},{4,2},{6,4},{8,6},{10,8},{12,10},{14,12},{16,14},{18,16},{20... | collective-permute-start | bytes 98312 | tf_op jit(solution)/shard_map/ppermute | solution.py:21
  104.5 6.8 %collective-permute-start.9 = (f32[8,1,1024]{2,1,0:T(1,128)S(1)}, f32[8,1,1024]{2,1,0:T(1,128)S(1)}, u32[]{:S(2)}, u32[]{:S(2)}) collective-permute-start(f32[8,1,1024]{2,1,0:T(1,128)S(1)} %get-tuple-element.13), channel_id=1, source_target_pairs={{0,2},{2,4},{4,6},{6,8},{8,10},{10,12},{12,14},{14,16},{16,18},{18... | collective-permute-start | bytes 98312 | tf_op jit(solution)/shard_map/ppermute | solution.py:19
  113.2 43.4 %collective-permute-start.11 = (f32[8,64,1024]{2,1,0:T(8,128)S(1)}, f32[8,64,1024]{2,1,0:T(8,128)S(1)}, u32[]{:S(2)}, u32[]{:S(2)}) collective-permute-start(f32[8,64,1024]{2,1,0:T(8,128)S(1)} %multiply_add_fusion.6), channel_id=1, source_target_pairs={{0,32},{32,64},{64,96},{1,33},{33,65},{65,97},{2,34},{34,66},{66,9... | collective-permute-start | bytes 6291464 | tf_op jit(solution)/shard_map/ppermute | solution.py:31
  156.7 6.1 collective-permute-start.12
  160.7 5.8 collective-permute-start.13
  166.5 9.3 %copy-start.12 = (s32[1,64]{1,0:T(1,128)S(1)}, s32[1,64]{1,0:T(1,128)}, u32[]{:S(2)}) copy-start(s32[1,64]{1,0:T(1,128)} %param.16) | copy-start | bytes 772
  166.5 9.4 %copy-start.13 = (f32[1,64]{1,0:T(1,128)S(1)}, f32[1,64]{1,0:T(1,128)}, u32[]{:S(2)}) copy-start(f32[1,64]{1,0:T(1,128)} %param.19) | copy-start | bytes 772
  169.5 41.1 %collective-permute-start.14 = (f32[8,64,1024]{2,1,0:T(8,128)}, f32[8,64,1024]{2,1,0:T(8,128)S(1)}, u32[]{:S(2)}, u32[]{:S(2)}) collective-permute-start(f32[8,64,1024]{2,1,0:T(8,128)} %multiply_add_fusion.5), channel_id=1, source_target_pairs={{0,32},{32,64},{64,96},{1,33},{33,65},{65,97},{2,34},{34,66},{66,9... | collective-permute-start | bytes 6291464 | tf_op jit(solution)/shard_map/ppermute | solution.py:31
  210.6 7.6 %collective-permute-start.15 = (f32[8,1,1024]{2,1,0:T(1,128)S(1)}, f32[8,1,1024]{2,1,0:T(1,128)S(1)}, u32[]{:S(2)}, u32[]{:S(2)}) collective-permute-start(f32[8,1,1024]{2,1,0:T(1,128)S(1)} %get-tuple-element.5), channel_id=1, source_target_pairs={{0,2},{2,4},{4,6},{6,8},{8,10},{10,12},{12,14},{14,16},{16,18},{18... | collective-permute-start | bytes 98312 | tf_op jit(solution)/shard_map/ppermute | solution.py:19
  216.0 7.8 %copy-start.2 = (f32[8,64,1024]{2,1,0:T(8,128)S(1)}, f32[8,64,1024]{2,1,0:T(8,128)}, u32[]{:S(2)}) copy-start(f32[8,64,1024]{2,1,0:T(8,128)} %copy-done.1) | copy-start | bytes 6291460
  216.1 7.8 %collective-permute-start.16 = (f32[8,1,1024]{2,1,0:T(1,128)S(1)}, f32[8,1,1024]{2,1,0:T(1,128)S(1)}, u32[]{:S(2)}, u32[]{:S(2)}) collective-permute-start(f32[8,1,1024]{2,1,0:T(1,128)S(1)} %get-tuple-element.4), channel_id=1, source_target_pairs={{2,0},{4,2},{6,4},{8,6},{10,8},{12,10},{14,12},{16,14},{18,16},{20... | collective-permute-start | bytes 98312 | tf_op jit(solution)/shard_map/ppermute | solution.py:21
  226.7 31.1 %copy-start.10 = (f32[1,64,16]{1,2,0:T(8,128)S(1)}, f32[1,64,16]{1,2,0:T(8,128)}, u32[]{:S(2)}) copy-start(f32[1,64,16]{1,2,0:T(8,128)} %param.18) | copy-start | bytes 12292
  226.7 31.1 %copy-start.11 = (f32[1,64]{1,0:T(1,128)S(1)}, f32[1,64]{1,0:T(1,128)}, u32[]{:S(2)}) copy-start(f32[1,64]{1,0:T(1,128)} %param.17) | copy-start | bytes 772
  (7 other events, 47.6 us)
where the time goes:
time: 610 us; the launch traced here: 609 us
  blocking collectives  349 us (57%)
  waiting for transfers between devices  135 us (22%)
  starting transfers between devices  54.3 us (9%)
  local copies, waits for them, and re-layouts  43 us (7%)
  other arithmetic  24.3 us (4%)
    psum x1, blocking collectives, per_device(): gram, cross = lax.psum((gram, cross), ('tm', 'space'))  345 us
    ppermute x3, waiting for transfers between devices, shifted(): lax.ppermute(value, axis, [(source, source + steps) for source in range(f...  114 us
    ppermute x7, starting transfers between devices, with_halo(): lax.ppermute(tail, axis, [(i, (i + 1) % count) for i in range(ends)])  32.1 us
    ppermute x7, waiting for transfers between devices, with_halo(): lax.ppermute(head, axis, [((i + 1) % count, i) for i in range(ends)])  21.2 us
    add x1, local copies, waits for them, and re-layouts, per_device(): running = correction + advance(padded, coeffs, own_rows, coarse_dt, None)  17.9 us
    ppermute x3, starting transfers between devices, shifted(): lax.ppermute(value, axis, [(source, source + steps) for source in range(f...  12.7 us
  transfers between devices with their start and end apart: 17, of which 9 were waited for; matrix products, arithmetic and copies ran while one was open for 2% of the time, Pallas kernels for 0%

commit v1 on v0

--- a/solution.py
+++ b/solution.py
@@ -105,7 +105,7 @@
     misfit = (obs_data[0][None, :] + obs_noise[0].T - every_pred) * inv_spread
     gram = jnp.dot(anomaly, anomaly.T, precision=lax.Precision.HIGHEST)
     cross = jnp.dot(anomaly, misfit.T, precision=lax.Precision.HIGHEST)
-    gram, cross = lax.psum((gram, cross), ("tm", "space"))
+    gram, cross = lax.psum(lax.psum((gram, cross), "tm"), "space")
     system = jnp.eye(total, dtype=jnp.float32) + gram
     factor = jnp.linalg.cholesky(system)
     weights = jax.scipy.linalg.cho_solve((factor, True), cross)

time: 610 us -> 355 us (0.58)
  blocking collectives: 349 us -> 94.6 us
    psum x1 -> x2, blocking collectives: 345 us -> 91 us  [per_device(): gram, cross = lax.psum(lax.psum((gram, cross), 'tm'), 'space')]
  transfers between devices with their start and end apart: 17 -> 17, of which waited for: 9 -> 9; matrix products, arithmetic and copies ran while one was open for 2% -> 4% of each run, Pallas kernels for 0% -> 0%
where the time goes in v1:
time: 355 us; the launch traced here: 354 us
  waiting for transfers between devices  135 us (38%)
  blocking collectives  94.6 us (27%)
  starting transfers between devices  54.3 us (15%)
  local copies, waits for them, and re-layouts  43.1 us (12%)
  other arithmetic  24.3 us (7%)
    ppermute x3, waiting for transfers between devices, shifted(): lax.ppermute(value, axis, [(source, source + steps) for source in range(f...  114 us
    psum x2, blocking collectives, per_device(): gram, cross = lax.psum(lax.psum((gram, cross), 'tm'), 'space')  91 us
    ppermute x7, starting transfers between devices, with_halo(): lax.ppermute(tail, axis, [(i, (i + 1) % count) for i in range(ends)])  32.1 us
    ppermute x7, waiting for transfers between devices, with_halo(): lax.ppermute(head, axis, [((i + 1) % count, i) for i in range(ends)])  21.2 us
    add x1, local copies, waits for them, and re-layouts, per_device(): running = correction + advance(padded, coeffs, own_rows, coarse_dt, None)  18 us
    ppermute x3, starting transfers between devices, shifted(): lax.ppermute(value, axis, [(source, source + steps) for source in range(f...  12.7 us
    gather x1, local copies, waits for them, and re-layouts, per_device(): predicted = jnp.take(flat, local_cell, axis=1)  11.1 us
    slice x7, local copies, waits for them, and re-layouts, advance(): west_cell = jnp.pad(middle[:, :, :-1], ((0, 0), (0, 0), (1, 0)))  10.1 us
  transfers between devices with their start and end apart: 17, of which 9 were waited for; matrix products, arithmetic and copies ran while one was open for 4% of the time, Pallas kernels for 0%

profile of v1, /device:TPU:0, one launch (start us, length us, event | category | flops | bytes accessed | tf_op | source)
XLA Modules:
  0.0 354.4 jit_solution(2229672048806556619)
XLA Ops:
  1.7 3.6 %collective-permute-start = (f32[8,1,1024]{2,1,0:T(1,128)S(1)}, f32[8,1,1024]{2,1,0:T(1,128)S(1)}, u32[]{:S(2)}, u32[]{:S(2)}) collective-permute-start(f32[8,1,1024]{2,1,0:T(1,128)S(1)} %get-tuple-element.33), channel_id=1, source_target_pairs={{0,2},{2,4},{4,6},{6,8},{8,10},{10,12},{12,14},{14,16},{16,18},{18... | collective-permute-start | bytes 98312 | tf_op jit(solution)/shard_map/ppermute | solution.py:19
  6.7 5.1 %fusion.52 = (f32[8,64,1023]{2,1,0:T(8,128)}, f32[8,64,1023]{2,1,0:T(8,128)}) fusion(f32[8,64,1024]{2,1,0:T(8,128)} %bitcast.40), kind=kLoop, calls=%fused_computation.96 | loop fusion | bytes 8380416 | tf_op jit(solution)/shard_map/slice | solution.py:38
  17.7 4.5 %collective-permute-start.2 = (f32[8,1,1024]{2,1,0:T(1,128)S(1)}, f32[8,1,1024]{2,1,0:T(1,128)S(1)}, u32[]{:S(2)}, u32[]{:S(2)}) collective-permute-start(f32[8,1,1024]{2,1,0:T(1,128)S(1)} %get-tuple-element.27), channel_id=1, source_target_pairs={{0,2},{2,4},{4,6},{6,8},{8,10},{10,12},{12,14},{14,16},{16,18},{18... | collective-permute-start | bytes 98312 | tf_op jit(solution)/shard_map/ppermute | solution.py:19
  24.4 3.7 %collective-permute-done.3 = f32[8,1,1024]{2,1,0:T(1,128)S(1)} collective-permute-done((f32[8,1,1024]{2,1,0:T(1,128)S(1)}, f32[8,1,1024]{2,1,0:T(1,128)S(1)}, u32[]{:S(2)}, u32[]{:S(2)}) %collective-permute-start.3) | collective-permute-done | bytes 32800 | tf_op jit(solution)/shard_map/ppermute | solution.py:21
  30.2 3.5 collective-permute-start.4
  35.8 4.6 %collective-permute-done.5 = f32[8,1,1024]{2,1,0:T(1,128)S(1)} collective-permute-done((f32[8,1,1024]{2,1,0:T(1,128)S(1)}, f32[8,1,1024]{2,1,0:T(1,128)S(1)}, u32[]{:S(2)}, u32[]{:S(2)}) %collective-permute-start.5) | collective-permute-done | bytes 32800 | tf_op jit(solution)/shard_map/ppermute | solution.py:21
  42.6 6.0 %collective-permute-start.6 = (f32[8,1,1024]{2,1,0:T(1,128)S(1)}, f32[8,1,1024]{2,1,0:T(1,128)S(1)}, u32[]{:S(2)}, u32[]{:S(2)}) collective-permute-start(f32[8,1,1024]{2,1,0:T(1,128)S(1)} %get-tuple-element.19), channel_id=1, source_target_pairs={{0,2},{2,4},{4,6},{6,8},{8,10},{10,12},{12,14},{14,16},{16,18},{18... | collective-permute-start | bytes 98312 | tf_op jit(solution)/shard_map/ppermute | solution.py:19
  51.0 3.7 %collective-permute-done.7 = f32[8,1,1024]{2,1,0:T(1,128)S(1)} collective-permute-done((f32[8,1,1024]{2,1,0:T(1,128)S(1)}, f32[8,1,1024]{2,1,0:T(1,128)S(1)}, u32[]{:S(2)}, u32[]{:S(2)}) %collective-permute-start.7) | collective-permute-done | bytes 32800 | tf_op jit(solution)/shard_map/ppermute | solution.py:21
  54.7 4.7 %subtract_select_fusion = f32[8,64,1024]{2,1,0:T(8,128)S(1)} fusion(f32[8,64,1024]{2,1,0:T(8,128)S(1)} %fusion.8, f32[8,64,1024]{2,1,0:T(8,128)S(1)} %bitcast.42, f32[8,64,1023]{2,1,0:T(8,128)S(1)} %get-tuple-element.21, f32[8,64,1023]{2,1,0:T(8,128)S(1)} %get-tuple-element.20, f32[8,1,1024]{2,1,0:T(1,128)S(1)} %collective-permute-done.6, ...), kind=kLoop, calls=%fused_computation.5 | loop fusion | flops 21495808 | bytes 15884545 | tf_op jit(solution)/shard_map/jit(_where)/select_n | solution.py:86
  59.4 3.5 collective-permute-start.8
  63.0 40.2 %collective-permute-done.8 = f32[8,64,1024]{2,1,0:T(8,128)S(1)} collective-permute-done((f32[8,64,1024]{2,1,0:T(8,128)S(1)}, f32[8,64,1024]{2,1,0:T(8,128)S(1)}, u32[]{:S(2)}, u32[]{:S(2)}) %collective-permute-start.8) | collective-permute-done | bytes 2097184 | tf_op jit(solution)/shard_map/ppermute | solution.py:31
  104.5 5.2 %collective-permute-start.9 = (f32[8,1,1024]{2,1,0:T(1,128)S(1)}, f32[8,1,1024]{2,1,0:T(1,128)S(1)}, u32[]{:S(2)}, u32[]{:S(2)}) collective-permute-start(f32[8,1,1024]{2,1,0:T(1,128)S(1)} %get-tuple-element.15), channel_id=1, source_target_pairs={{0,2},{2,4},{4,6},{6,8},{8,10},{10,12},{12,14},{14,16},{16,18},{18... | collective-permute-start | bytes 98312 | tf_op jit(solution)/shard_map/ppermute | solution.py:19
  113.2 4.7 %collective-permute-start.11 = (f32[8,64,1024]{2,1,0:T(8,128)S(1)}, f32[8,64,1024]{2,1,0:T(8,128)S(1)}, u32[]{:S(2)}, u32[]{:S(2)}) collective-permute-start(f32[8,64,1024]{2,1,0:T(8,128)S(1)} %multiply_add_fusion.6), channel_id=1, source_target_pairs={{0,32},{32,64},{64,96},{1,33},{33,65},{65,97},{2,34},{34,66},{66,9... | collective-permute-start | bytes 6291464 | tf_op jit(solution)/shard_map/ppermute | solution.py:31
  118.0 38.7 %collective-permute-done.11 = f32[8,64,1024]{2,1,0:T(8,128)S(1)} collective-permute-done((f32[8,64,1024]{2,1,0:T(8,128)S(1)}, f32[8,64,1024]{2,1,0:T(8,128)S(1)}, u32[]{:S(2)}, u32[]{:S(2)}) %collective-permute-start.11) | collective-permute-done | bytes 2097184 | tf_op jit(solution)/shard_map/ppermute | solution.py:31
  156.7 3.9 %collective-permute-start.12 = (f32[8,1,1024]{2,1,0:T(1,128)S(1)}, f32[8,1,1024]{2,1,0:T(1,128)S(1)}, u32[]{:S(2)}, u32[]{:S(2)}) collective-permute-start(f32[8,1,1024]{2,1,0:T(1,128)S(1)} %get-tuple-element.11), channel_id=1, source_target_pairs={{0,2},{2,4},{4,6},{6,8},{8,10},{10,12},{12,14},{14,16},{16,18},{18... | collective-permute-start | bytes 98312 | tf_op jit(solution)/shard_map/ppermute | solution.py:19
  162.8 3.7 %collective-permute-done.13 = f32[8,1,1024]{2,1,0:T(1,128)S(1)} collective-permute-done((f32[8,1,1024]{2,1,0:T(1,128)S(1)}, f32[8,1,1024]{2,1,0:T(1,128)S(1)}, u32[]{:S(2)}, u32[]{:S(2)}) %collective-permute-start.13) | collective-permute-done | bytes 32800 | tf_op jit(solution)/shard_map/ppermute | solution.py:21
  169.5 4.5 %collective-permute-start.14 = (f32[8,64,1024]{2,1,0:T(8,128)}, f32[8,64,1024]{2,1,0:T(8,128)S(1)}, u32[]{:S(2)}, u32[]{:S(2)}) collective-permute-start(f32[8,64,1024]{2,1,0:T(8,128)} %multiply_add_fusion.5), channel_id=1, source_target_pairs={{0,32},{32,64},{64,96},{1,33},{33,65},{65,97},{2,34},{34,66},{66,9... | collective-permute-start | bytes 6291464 | tf_op jit(solution)/shard_map/ppermute | solution.py:31
  175.9 34.7 %collective-permute-done.14 = f32[8,64,1024]{2,1,0:T(8,128)S(1)} collective-permute-done((f32[8,64,1024]{2,1,0:T(8,128)}, f32[8,64,1024]{2,1,0:T(8,128)S(1)}, u32[]{:S(2)}, u32[]{:S(2)}) %collective-permute-start.14) | collective-permute-done | bytes 2097184 | tf_op jit(solution)/shard_map/ppermute | solution.py:31
  210.6 5.4 %collective-permute-start.15 = (f32[8,1,1024]{2,1,0:T(1,128)S(1)}, f32[8,1,1024]{2,1,0:T(1,128)S(1)}, u32[]{:S(2)}, u32[]{:S(2)}) collective-permute-start(f32[8,1,1024]{2,1,0:T(1,128)S(1)} %get-tuple-element.7), channel_id=1, source_target_pairs={{0,2},{2,4},{4,6},{6,8},{8,10},{10,12},{12,14},{14,16},{16,18},{18... | collective-permute-start | bytes 98312 | tf_op jit(solution)/shard_map/ppermute | solution.py:19
  218.2 5.6 %collective-permute-done.16 = f32[8,1,1024]{2,1,0:T(1,128)S(1)} collective-permute-done((f32[8,1,1024]{2,1,0:T(1,128)S(1)}, f32[8,1,1024]{2,1,0:T(1,128)S(1)}, u32[]{:S(2)}, u32[]{:S(2)}) %collective-permute-start.16) | collective-permute-done | bytes 32800 | tf_op jit(solution)/shard_map/ppermute | solution.py:21
  226.7 18.0 %copy.18 = f32[8,64,1024]{0,2,1:T(8,128)} copy(f32[8,64,1024]{2,1,0:T(8,128)} %multiply_add_fusion.4) | data formatting | bytes 4194304 | tf_op jit(solution)/shard_map/add | solution.py:91
  244.7 11.1 %gather_fusion = f32[64,8]{1,0:T(8,128)S(1)} fusion(f32[8,65536]{0,1:T(8,128)} %bitcast.43, s32[1024]{0:T(1024)S(1)} %pad_clamp_fusion), kind=kCustom, calls=%fused_computation | custom fusion | bytes 4352 | tf_op jit(solution)/shard_map/jit(_take)/gather | solution.py:95
  258.1 17.8 %all-reduce.15 = (f32[16,16]{1,0:T(8,128)S(1)}, f32[16,16]{1,0:T(8,128)S(1)}) all-reduce(f32[16,16]{1,0:T(8,128)S(1)} %fusion.21, f32[16,16]{1,0:T(8,128)S(1)} %fusion.29), channel_id=1, replica_groups=mesh['tm'=4,'space'=16,'ens'=2] {'tm'}, use_global_device_ids=true, to_apply=%region_5.6 | all-reduce | flops 512 | bytes 4096 | tf_op jit(solution)/shard_map/psum | solution.py:108
  275.9 73.2 %all-reduce.14 = (f32[16,16]{1,0:T(8,128)S(1)}, f32[16,16]{1,0:T(8,128)S(1)}) all-reduce(f32[16,16]{1,0:T(8,128)S(1)} %get-tuple-element.4, f32[16,16]{1,0:T(8,128)S(1)} %get-tuple-element.5), channel_id=1, replica_groups=mesh['tm'=4,'space'=16,'ens'=2] {'space'}, use_global_device_ids=true, to_apply=%region_6.7 | all-reduce | flops 512 | bytes 4096 | tf_op jit(solution)/shard_map/psum | solution.py:108
  (91 shorter events, 43.6 us)
Async XLA Ops:
  1.7 12.4 %collective-permute-start = (f32[8,1,1024]{2,1,0:T(1,128)S(1)}, f32[8,1,1024]{2,1,0:T(1,128)S(1)}, u32[]{:S(2)}, u32[]{:S(2)}) collective-permute-start(f32[8,1,1024]{2,1,0:T(1,128)S(1)} %get-tuple-element.33), channel_id=1, source_target_pairs={{0,2},{2,4},{4,6},{6,8},{8,10},{10,12},{12,14},{14,16},{16,18},{18... | collective-permute-start | bytes 98312 | tf_op jit(solution)/shard_map/ppermute | solution.py:19
  5.3 8.9 %collective-permute-start.1 = (f32[8,1,1024]{2,1,0:T(1,128)S(1)}, f32[8,1,1024]{2,1,0:T(1,128)S(1)}, u32[]{:S(2)}, u32[]{:S(2)}) collective-permute-start(f32[8,1,1024]{2,1,0:T(1,128)S(1)} %get-tuple-element.32), channel_id=1, source_target_pairs={{2,0},{4,2},{6,4},{8,6},{10,8},{12,10},{14,12},{16,14},{18,16},{20... | collective-permute-start | bytes 98312 | tf_op jit(solution)/shard_map/ppermute | solution.py:21
  6.6 7.6 %copy-start = (f32[1,8,64,1024]{3,2,1,0:T(8,128)S(1)}, f32[1,8,64,1024]{3,2,1,0:T(8,128)}, u32[]{:S(2)}) copy-start(f32[1,8,64,1024]{3,2,1,0:T(8,128)} %param.10) | copy-start | bytes 6291460
  17.7 6.7 %collective-permute-start.2 = (f32[8,1,1024]{2,1,0:T(1,128)S(1)}, f32[8,1,1024]{2,1,0:T(1,128)S(1)}, u32[]{:S(2)}, u32[]{:S(2)}) collective-permute-start(f32[8,1,1024]{2,1,0:T(1,128)S(1)} %get-tuple-element.27), channel_id=1, source_target_pairs={{0,2},{2,4},{4,6},{6,8},{8,10},{10,12},{12,14},{14,16},{16,18},{18... | collective-permute-start | bytes 98312 | tf_op jit(solution)/shard_map/ppermute | solution.py:19
  22.3 5.8 %collective-permute-start.3 = (f32[8,1,1024]{2,1,0:T(1,128)S(1)}, f32[8,1,1024]{2,1,0:T(1,128)S(1)}, u32[]{:S(2)}, u32[]{:S(2)}) collective-permute-start(f32[8,1,1024]{2,1,0:T(1,128)S(1)} %get-tuple-element.26), channel_id=1, source_target_pairs={{2,0},{4,2},{6,4},{8,6},{10,8},{12,10},{14,12},{16,14},{18,16},{20... | collective-permute-start | bytes 98312 | tf_op jit(solution)/shard_map/ppermute | solution.py:21
  30.2 5.6 %collective-permute-start.4 = (f32[8,1,1024]{2,1,0:T(1,128)S(1)}, f32[8,1,1024]{2,1,0:T(1,128)S(1)}, u32[]{:S(2)}, u32[]{:S(2)}) collective-permute-start(f32[8,1,1024]{2,1,0:T(1,128)S(1)} %get-tuple-element.23), channel_id=1, source_target_pairs={{0,2},{2,4},{4,6},{6,8},{8,10},{10,12},{12,14},{14,16},{16,18},{18... | collective-permute-start | bytes 98312 | tf_op jit(solution)/shard_map/ppermute | solution.py:19
  33.7 6.8 %collective-permute-start.5 = (f32[8,1,1024]{2,1,0:T(1,128)S(1)}, f32[8,1,1024]{2,1,0:T(1,128)S(1)}, u32[]{:S(2)}, u32[]{:S(2)}) collective-permute-start(f32[8,1,1024]{2,1,0:T(1,128)S(1)} %get-tuple-element.22), channel_id=1, source_target_pairs={{2,0},{4,2},{6,4},{8,6},{10,8},{12,10},{14,12},{16,14},{18,16},{20... | collective-permute-start | bytes 98312 | tf_op jit(solution)/shard_map/ppermute | solution.py:21
  42.6 8.5 %collective-permute-start.6 = (f32[8,1,1024]{2,1,0:T(1,128)S(1)}, f32[8,1,1024]{2,1,0:T(1,128)S(1)}, u32[]{:S(2)}, u32[]{:S(2)}) collective-permute-start(f32[8,1,1024]{2,1,0:T(1,128)S(1)} %get-tuple-element.19), channel_id=1, source_target_pairs={{0,2},{2,4},{4,6},{6,8},{8,10},{10,12},{12,14},{14,16},{16,18},{18... | collective-permute-start | bytes 98312 | tf_op jit(solution)/shard_map/ppermute | solution.py:19
  48.6 6.1 %collective-permute-start.7 = (f32[8,1,1024]{2,1,0:T(1,128)S(1)}, f32[8,1,1024]{2,1,0:T(1,128)S(1)}, u32[]{:S(2)}, u32[]{:S(2)}) collective-permute-start(f32[8,1,1024]{2,1,0:T(1,128)S(1)} %get-tuple-element.18), channel_id=1, source_target_pairs={{2,0},{4,2},{6,4},{8,6},{10,8},{12,10},{14,12},{16,14},{18,16},{20... | collective-permute-start | bytes 98312 | tf_op jit(solution)/shard_map/ppermute | solution.py:21
  59.4 107.1 %copy-start.1 = (f32[8,64,1024]{2,1,0:T(8,128)}, f32[8,64,1024]{2,1,0:T(8,128)S(1)}, u32[]{:S(2)}) copy-start(f32[8,64,1024]{2,1,0:T(8,128)S(1)} %subtract_select_fusion) | copy-start | bytes 6291460
  59.4 43.7 %collective-permute-start.8 = (f32[8,64,1024]{2,1,0:T(8,128)S(1)}, f32[8,64,1024]{2,1,0:T(8,128)S(1)}, u32[]{:S(2)}, u32[]{:S(2)}) collective-permute-start(f32[8,64,1024]{2,1,0:T(8,128)S(1)} %subtract_select_fusion), channel_id=1, source_target_pairs={{0,32},{32,64},{64,96},{1,33},{33,65},{65,97},{2,34},{34,66},{66,9... | collective-permute-start | bytes 6291464 | tf_op jit(solution)/shard_map/ppermute | solution.py:31
  103.2 7.3 %collective-permute-start.10 = (f32[8,1,1024]{2,1,0:T(1,128)S(1)}, f32[8,1,1024]{2,1,0:T(1,128)S(1)}, u32[]{:S(2)}, u32[]{:S(2)}) collective-permute-start(f32[8,1,1024]{2,1,0:T(1,128)S(1)} %get-tuple-element.14), channel_id=1, source_target_pairs={{2,0},{4,2},{6,4},{8,6},{10,8},{12,10},{14,12},{16,14},{18,16},{20... | collective-permute-start | bytes 98312 | tf_op jit(solution)/shard_map/ppermute | solution.py:21
  104.5 6.8 %collective-permute-start.9 = (f32[8,1,1024]{2,1,0:T(1,128)S(1)}, f32[8,1,1024]{2,1,0:T(1,128)S(1)}, u32[]{:S(2)}, u32[]{:S(2)}) collective-permute-start(f32[8,1,1024]{2,1,0:T(1,128)S(1)} %get-tuple-element.15), channel_id=1, source_target_pairs={{0,2},{2,4},{4,6},{6,8},{8,10},{10,12},{12,14},{14,16},{16,18},{18... | collective-permute-start | bytes 98312 | tf_op jit(solution)/shard_map/ppermute | solution.py:19
  113.2 43.4 %collective-permute-start.11 = (f32[8,64,1024]{2,1,0:T(8,128)S(1)}, f32[8,64,1024]{2,1,0:T(8,128)S(1)}, u32[]{:S(2)}, u32[]{:S(2)}) collective-permute-start(f32[8,64,1024]{2,1,0:T(8,128)S(1)} %multiply_add_fusion.6), channel_id=1, source_target_pairs={{0,32},{32,64},{64,96},{1,33},{33,65},{65,97},{2,34},{34,66},{66,9... | collective-permute-start | bytes 6291464 | tf_op jit(solution)/shard_map/ppermute | solution.py:31
  156.7 6.1 %collective-permute-start.12 = (f32[8,1,1024]{2,1,0:T(1,128)S(1)}, f32[8,1,1024]{2,1,0:T(1,128)S(1)}, u32[]{:S(2)}, u32[]{:S(2)}) collective-permute-start(f32[8,1,1024]{2,1,0:T(1,128)S(1)} %get-tuple-element.11), channel_id=1, source_target_pairs={{0,2},{2,4},{4,6},{6,8},{8,10},{10,12},{12,14},{14,16},{16,18},{18... | collective-permute-start | bytes 98312 | tf_op jit(solution)/shard_map/ppermute | solution.py:19
  160.7 5.8 %collective-permute-start.13 = (f32[8,1,1024]{2,1,0:T(1,128)S(1)}, f32[8,1,1024]{2,1,0:T(1,128)S(1)}, u32[]{:S(2)}, u32[]{:S(2)}) collective-permute-start(f32[8,1,1024]{2,1,0:T(1,128)S(1)} %get-tuple-element.10), channel_id=1, source_target_pairs={{2,0},{4,2},{6,4},{8,6},{10,8},{12,10},{14,12},{16,14},{18,16},{20... | collective-permute-start | bytes 98312 | tf_op jit(solution)/shard_map/ppermute | solution.py:21
  166.5 9.3 %copy-start.12 = (s32[1,64]{1,0:T(1,128)S(1)}, s32[1,64]{1,0:T(1,128)}, u32[]{:S(2)}) copy-start(s32[1,64]{1,0:T(1,128)} %param.16) | copy-start | bytes 772
  166.5 9.4 %copy-start.13 = (f32[1,64]{1,0:T(1,128)S(1)}, f32[1,64]{1,0:T(1,128)}, u32[]{:S(2)}) copy-start(f32[1,64]{1,0:T(1,128)} %param.19) | copy-start | bytes 772
  169.5 41.1 %collective-permute-start.14 = (f32[8,64,1024]{2,1,0:T(8,128)}, f32[8,64,1024]{2,1,0:T(8,128)S(1)}, u32[]{:S(2)}, u32[]{:S(2)}) collective-permute-start(f32[8,64,1024]{2,1,0:T(8,128)} %multiply_add_fusion.5), channel_id=1, source_target_pairs={{0,32},{32,64},{64,96},{1,33},{33,65},{65,97},{2,34},{34,66},{66,9... | collective-permute-start | bytes 6291464 | tf_op jit(solution)/shard_map/ppermute | solution.py:31
  210.6 7.6 %collective-permute-start.15 = (f32[8,1,1024]{2,1,0:T(1,128)S(1)}, f32[8,1,1024]{2,1,0:T(1,128)S(1)}, u32[]{:S(2)}, u32[]{:S(2)}) collective-permute-start(f32[8,1,1024]{2,1,0:T(1,128)S(1)} %get-tuple-element.7), channel_id=1, source_target_pairs={{0,2},{2,4},{4,6},{6,8},{8,10},{10,12},{12,14},{14,16},{16,18},{18... | collective-permute-start | bytes 98312 | tf_op jit(solution)/shard_map/ppermute | solution.py:19
  216.0 7.8 %copy-start.2 = (f32[8,64,1024]{2,1,0:T(8,128)S(1)}, f32[8,64,1024]{2,1,0:T(8,128)}, u32[]{:S(2)}) copy-start(f32[8,64,1024]{2,1,0:T(8,128)} %copy-done.1) | copy-start | bytes 6291460
  216.1 7.8 %collective-permute-start.16 = (f32[8,1,1024]{2,1,0:T(1,128)S(1)}, f32[8,1,1024]{2,1,0:T(1,128)S(1)}, u32[]{:S(2)}, u32[]{:S(2)}) collective-permute-start(f32[8,1,1024]{2,1,0:T(1,128)S(1)} %get-tuple-element.6), channel_id=1, source_target_pairs={{2,0},{4,2},{6,4},{8,6},{10,8},{12,10},{14,12},{16,14},{18,16},{20... | collective-permute-start | bytes 98312 | tf_op jit(solution)/shard_map/ppermute | solution.py:21
  226.7 31.2 %copy-start.10 = (f32[1,64,16]{1,2,0:T(8,128)S(1)}, f32[1,64,16]{1,2,0:T(8,128)}, u32[]{:S(2)}) copy-start(f32[1,64,16]{1,2,0:T(8,128)} %param.18) | copy-start | bytes 12292
  226.7 31.2 %copy-start.11 = (f32[1,64]{1,0:T(1,128)S(1)}, f32[1,64]{1,0:T(1,128)}, u32[]{:S(2)}) copy-start(f32[1,64]{1,0:T(1,128)} %param.17) | copy-start | bytes 772
  (7 other events, 47.6 us)
